TPU v7x, 32 devices: a whole 2x2x4 slice. The times are simulated.
32 devices in a mesh: ep: 16 (over z, y, core), dp: 2 (over x).
Axes of the slice: x: 2, y: 2, z: 4, core: 2. Of those that a mesh axis runs over, the one named last changes fastest.
Arguments:
- moe_rows: bfloat16 [1024, 3584], P(('dp', 'ep')), parts along dimension 0, may hold values from -6 to 6
- routes: int32 [1024, 4], P(('dp', 'ep')), parts along dimension 0, may hold values from 0 to 7, all different within a row; in each aligned block of 32 rows (0 to 31, 32 to 63, ...) at most 32 rows name the same one
- route_weights: float32 [1024, 4], P(('dp', 'ep')), parts along dimension 0, may hold values from 0.05 to 0.5
- w_gate: bfloat16 [16, 3584, 512], P('ep'), may hold values from -0.09375 to 0.09375
- w_up: bfloat16 [16, 3584, 512], P('ep'), may hold values from -0.09375 to 0.09375
- w_down: bfloat16 [16, 512, 3584], P('ep'), may hold values from -0.1875 to 0.1875
- queries: bfloat16 [128, 64, 576], P(('dp', 'ep')), parts along dimension 0, may hold values from -45 to 45
- latent_cache: bfloat16 [128, 128, 576], P(('dp', 'ep')), parts along dimension 0, may hold values from -6 to 6
- lengths: int32 [128], P(('dp', 'ep')), parts along dimension 0, may hold values from 2 to 128, as said below
Outputs:
- moe_out: bfloat16 [1024, 3584], P(('dp', 'ep')), parts along dimension 0
- attn_out: bfloat16 [128, 64, 512], P(('dp', 'ep')), parts along dimension 0
There are 2 independent parts, one for each index of `dp`. A program takes and returns all parts, laid end to end along the dimension named above; an argument that names none is the same for every part. Nothing has to cross between parts.
Inputs may be any that keep to these rules, and one draw needn't show every extreme that they name: `routes`: each row names 4 different experts; in each aligned block of 32 rows (the rows of one device) no expert is named by more than 32 rows, a bound that some block reaches. `lengths`: some row of every part uses all 128 positions.
All inputs are finite; a program needn't handle non-finite values.
Results may differ from a plain program's by a relative error of at most 0.0085.
Values may be sent and summed in bfloat16 or wider, within the bound.
No kernel may reach another device: no remote copies, remote signals or barrier semaphores. Data moves between devices by JAX's collectives and lax.ppermute only.
A program may use at most 128 MiB of HBM per device.

v0:
```python
import jax
import jax.numpy as jnp
from jax import lax
from jax.sharding import PartitionSpec as P

LATENT = 512
score_scale = 192.0 ** (-0.5)


def attend(queries, latent_cache, lengths):
    scores = (
        jnp.einsum("rhc,rlc->rhl", queries, latent_cache, preferred_element_type=jnp.float32)
        * score_scale
    )
    in_range = (
        jnp.arange(latent_cache.shape[1], dtype=jnp.int32)[None, None, :] < lengths[:, None, None]
    )
    scores = jnp.where(in_range, scores, -1e30)
    highest = jnp.max(scores, axis=-1, keepdims=True)
    expo = jnp.where(in_range, jnp.exp(scores - highest), 0.0)
    probs = (expo / jnp.sum(expo, axis=-1, keepdims=True)).astype(jnp.bfloat16)
    return jnp.einsum(
        "rhl,rlc->rhc", probs, latent_cache[:, :, :LATENT], preferred_element_type=jnp.float32
    ).astype(jnp.bfloat16)


def shards(moe_rows, routes, route_weights, w_gate, w_up, w_down, queries, latent_cache, lengths):
    attn_out = attend(queries, latent_cache, lengths)
    rows_here, model_width = moe_rows.shape
    experts = lax.axis_size("ep") // 2
    expert = lax.axis_index("ep") // 2
    named = routes[:, :, None] == jnp.arange(experts, dtype=jnp.int32)[None, None, :]
    dense_w = jnp.sum(jnp.where(named, route_weights[:, :, None], 0.0), axis=1)
    hi = dense_w.astype(jnp.bfloat16)
    rest = dense_w - hi.astype(jnp.float32)
    mid = rest.astype(jnp.bfloat16)
    lo = (rest - mid.astype(jnp.float32)).astype(jnp.bfloat16)
    extra = -(-3 * experts // 128) * 128
    tail = jnp.zeros((rows_here, extra - 3 * experts), jnp.bfloat16)
    packed = jnp.concatenate([moe_rows, hi, mid, lo, tail], axis=1)
    gathered = lax.all_gather(packed, "ep", axis=0, tiled=True)
    all_rows = gathered[:, :model_width]
    parts = gathered[:, model_width : model_width + 3 * experts].astype(jnp.float32)
    parts = parts.reshape(-1, 3, experts)
    weight_all = parts[:, 0] + (parts[:, 1] + parts[:, 2])
    weight = jnp.sum(jnp.where(jnp.arange(experts)[None, :] == expert, weight_all, 0.0), axis=1)
    gate_act = jnp.dot(all_rows, w_gate[0], preferred_element_type=jnp.float32)
    up_act = jnp.dot(all_rows, w_up[0], preferred_element_type=jnp.float32)
    hidden = (jax.nn.silu(gate_act) * up_act).astype(jnp.bfloat16)
    partial_out = jnp.dot(hidden, w_down[0], preferred_element_type=jnp.float32)
    partial_out = partial_out * weight[:, None]
    moe_out = lax.psum_scatter(partial_out, "ep", scatter_dimension=0, tiled=True)
    return (moe_out.astype(jnp.bfloat16), attn_out)


def solution(mesh):
    in_specs = (
        P(("dp", "ep"), None),
        P(("dp", "ep"), None),
        P(("dp", "ep"), None),
        P("ep", None, None),
        P("ep", None, None),
        P("ep", None, None),
        P(("dp", "ep"), None, None),
        P(("dp", "ep"), None, None),
        P(("dp", "ep")),
    )
    out_specs = (P(("dp", "ep"), None), P(("dp", "ep"), None, None))
    return jax.shard_map(shards, mesh=mesh, in_specs=in_specs, out_specs=out_specs, check_vma=False)
```

profile of v0, /device:TPU:0, one launch (start us, length us, event | category | flops | bytes accessed | tf_op | source)
XLA Modules:
  0.0 178.8 jit_solution(15685329627394911693)
XLA Ops:
  7.2 0.0 copy-start
  7.2 0.0 all-gather.2.cloned.1.call-start
  7.2 0.7 select_reduce_fusion
  8.0 0.1 copy.22
  8.1 0.1 copy.23
  8.2 0.1 copy.24
  8.3 1.7 concatenate.3
  10.0 0.0 all-gather.2.cloned.1.call-update
  10.0 0.0 reduce-scatter.2.cloned.1.call-start
  10.1 51.7 %all-gather.2.cloned.1.call-done = bf16[512,3712]{1,0:T(8,128)(2,1)} async-done(((bf16[32,3712]{1,0:T(8,128)(2,1)}), bf16[512,3712]{1,0:T(8,128)(2,1)}) %all-gather.2.cloned.1.call-update) | async-done | bytes 3801104 | tf_op jit(solution)/shard_map/all_gather | solution.py:41
  61.7 0.9 slice.25
  62.6 0.1 copy.27
  62.7 0.1 fusion.32
  62.8 5.2 %fusion.4 = f32[512,512]{1,0:T(8,128)S(1)} fusion(bf16[1,3584,512]{2,1,0:T(8,128)(2,1)} %param.12, bf16[512,3712]{1,0:T(8,128)(2,1)} %all-gather.2.cloned.1.call-done), kind=kOutput, calls=%fused_computation.5 | convolution fusion | flops 1879048192 | bytes 8388608 | tf_op jit(solution)/shard_map/dot_general | solution.py:47
  68.0 11.2 %convolution_multiply_fusion = f32[512,3584]{1,0:T(8,128)} fusion(bf16[1,512,3584]{2,1,0:T(8,128)(2,1)} %param.14, f32[512]{0:T(512)S(1)} %fusion.32, bf16[1,3584,512]{2,1,0:T(8,128)(2,1)} %param.13, bf16[512,3712]{1,0:T(8,128)(2,1)} %all-gather.2.cloned.1.call-done, f32[512,512]{1,0:T(8,128)S(1)} %fusion.4), kind=kOutput, calls=%fused_computation.1 | convolution fusion | flops 3761504256 | bytes 19400704 | tf_op jit(solution)/shard_map/dot_general | solution.py:50
  79.3 0.0 copy-start.2
  79.3 0.0 copy-start.1
  79.3 0.0 reduce-scatter.2.cloned.1.call-update
  79.3 0.6 copy-done.2
  79.9 0.1 iota_compare_fusion.1
  80.0 0.0 copy-done
  80.0 0.3 copy-done.1
  80.3 0.2 fusion.19
  80.6 0.2 fusion.37
  80.8 1.3 convolution_convert_fusion
  82.1 88.2 %reduce-scatter.2.cloned.1.call-done = f32[32,3584]{1,0:T(8,128)} async-done(((f32[512,3584]{1,0:T(8,128)}), f32[32,3584]{1,0:T(8,128)}) %reduce-scatter.2.cloned.1.call-update) | async-done | bytes 458768 | tf_op jit(solution)/shard_map/reduce_scatter | solution.py:52
  170.2 1.7 convert_element_type.34
  (4 shorter events, 0.0 us)
Async XLA Ops:
  7.2 72.8 %copy-start = (bf16[4,64,576]{2,1,0:T(8,128)(2,1)S(1)}, bf16[4,64,576]{2,1,0:T(8,128)(2,1)}, u32[]{:S(2)}) copy-start(bf16[4,64,576]{2,1,0:T(8,128)(2,1)} %param.15) | copy-start | bytes 884740
  7.2 54.6 %all-gather.2.cloned.1.call-start = ((), (), s32[]{:S(2)}) async-start(), calls=%async_computation.1 | async-start | bytes 4038656 | tf_op jit(solution)/shard_map/all_gather | solution.py:41
  10.0 160.2 %reduce-scatter.2.cloned.1.call-start = ((), (), s32[]{:S(2)}) async-start(), calls=%async_computation.2 | async-start | bytes 7798784 | tf_op jit(solution)/shard_map/reduce_scatter | solution.py:52
  79.3 0.7 copy-start.2
  79.3 1.1 copy-start.1
Sparse Core Ops, SparseCore 0:
  10.9 50.8 all-gather.1
  79.4 90.7 reduce-scatter.1
where the time goes:
time: 179 us
  waiting for transfers between devices  140 us (78%)
  matrix products  18 us (10%)
  between operations  14.1 us (8%)
  local copies, waits for them, and re-layouts  3.97 us (2%)
  other arithmetic  2.85 us (2%)
    reduce_scatter x1, waiting for transfers between devices, shards(): lax.psum_scatter(partial_out, 'ep', scatter_dimension=0, tiled=True)  88.2 us
    all_gather x1, waiting for transfers between devices, shards(): gathered = lax.all_gather(packed, 'ep', axis=0, tiled=True)  51.7 us
    dot_general x1, matrix products, shards(): partial_out = jnp.dot(hidden, w_down[0], preferred_element_type=jnp.float32)  11.2 us
    dot_general x1, matrix products, shards(): gate_act = jnp.dot(all_rows, w_gate[0], preferred_element_type=jnp.float32)  5.21 us
  transfers between devices with their start and end apart: 2, of which 2 were waited for; matrix products, arithmetic and copies ran while one was open for 1% of the time, Pallas kernels for 0%

commit v1 on v0

--- a/solution.py
+++ b/solution.py
@@ -38,7 +38,21 @@
     extra = -(-3 * experts // 128) * 128
     tail = jnp.zeros((rows_here, extra - 3 * experts), jnp.bfloat16)
     packed = jnp.concatenate([moe_rows, hi, mid, lo, tail], axis=1)
-    gathered = lax.all_gather(packed, "ep", axis=0, tiled=True)
+    ways, here, turn = (lax.axis_size("ep"), lax.axis_index("ep"), packed.shape[0])
+    shape = [n * ways if d == 0 else n for d, n in enumerate(packed.shape)]
+    full = lax.dynamic_update_slice_in_dim(
+        jnp.zeros(shape, packed.dtype), packed, here * turn, axis=0
+    )
+    going_up = going_down = packed
+    for far in range(1, ways // 2 + 1):
+        going_up = lax.ppermute(going_up, "ep", [(d, (d + 1) % ways) for d in range(ways)])
+        full = lax.dynamic_update_slice_in_dim(full, going_up, (here - far) % ways * turn, axis=0)
+        if 2 * far < ways:
+            going_down = lax.ppermute(going_down, "ep", [(d, (d - 1) % ways) for d in range(ways)])
+            full = lax.dynamic_update_slice_in_dim(
+                full, going_down, (here + far) % ways * turn, axis=0
+            )
+    gathered = full
     all_rows = gathered[:, :model_width]
     parts = gathered[:, model_width : model_width + 3 * experts].astype(jnp.float32)
     parts = parts.reshape(-1, 3, experts)

time: 179 us -> 377 us (2.11); the launches traced: 179 us -> 371 us
  local copies, waits for them, and re-layouts: 3.97 us -> 189 us
  starting transfers between devices: 0.08 us -> 32.3 us
  waiting for transfers between devices: 140 us -> 118 us
  matrix products: 18 us -> 14.1 us
    dynamic_update_slice x0 -> x16, local copies, waits for them, and re-layouts: none -> 176 us  [the longest x8 86.4 us: shards(): lax.dynamic_update_slice_in_dim(full, going_up, (here - far) % ways * tur...]
    all_gather x1 -> x0, waiting for transfers between devices: 51.7 us -> none  [shards(): gathered = lax.all_gather(packed, 'ep', axis=0, tiled=True)]
    ppermute x0 -> x15, starting transfers between devices: none -> 32.3 us  [the longest x7 31.8 us: shards(): lax.ppermute(going_down, 'ep', [(d, (d - 1) % ways) for d in range(ways)])]
    ppermute x0 -> x15, waiting for transfers between devices: none -> 27.1 us  [the longest x8 27.1 us: shards(): lax.ppermute(going_up, 'ep', [(d, (d + 1) % ways) for d in range(ways)])]
    ppermute x0 -> x15, local copies, waits for them, and re-layouts: none -> 8.66 us  [the longest x8 4.55 us: shards(): lax.ppermute(going_up, 'ep', [(d, (d + 1) % ways) for d in range(ways)])]
    dot_general x1, matrix products: 11.2 us -> 5.1 us  [shards(): partial_out = jnp.dot(hidden, w_down[0], preferred_element_type=jnp.float32)]
    dot_general x0 -> x1, matrix products: none -> 5.37 us  [shards(): up_act = jnp.dot(all_rows, w_up[0], preferred_element_type=jnp.float32)]
  transfers between devices with their start and end apart: 2 -> 16, of which waited for: 2 -> 8; matrix products, arithmetic and copies ran while one was open for 1% -> 48% of each run, Pallas kernels for 0% -> 0%
where the time goes in v1:
time: 377 us; the launch traced here: 371 us
  local copies, waits for them, and re-layouts  189 us (50%)
  waiting for transfers between devices  118 us (31%)
  starting transfers between devices  32.3 us (9%)
  between operations  14.5 us (4%)
  matrix products  14.1 us (4%)
    reduce_scatter x1, waiting for transfers between devices, shards(): lax.psum_scatter(partial_out, 'ep', scatter_dimension=0, tiled=True)  90.4 us
    dynamic_update_slice x8, local copies, waits for them, and re-layouts, shards(): lax.dynamic_update_slice_in_dim(full, going_up, (here - far) % ways * tur...  86.4 us
    dynamic_update_slice x7, local copies, waits for them, and re-layouts, shards(): lax.dynamic_update_slice_in_dim(full, going_down, (here + far) % ways * t...  79.3 us
    ppermute x7, starting transfers between devices, shards(): lax.ppermute(going_down, 'ep', [(d, (d - 1) % ways) for d in range(ways)])  31.8 us
    ppermute x8, waiting for transfers between devices, shards(): lax.ppermute(going_up, 'ep', [(d, (d + 1) % ways) for d in range(ways)])  27.1 us
    dynamic_update_slice x1, local copies, waits for them, and re-layouts, shards(): lax.dynamic_update_slice_in_dim(jnp.zeros(shape, packed.dtype), packed, h...  10 us
  transfers between devices with their start and end apart: 16, of which 8 were waited for; matrix products, arithmetic and copies ran while one was open for 48% of the time, Pallas kernels for 0%

profile of v1, /device:TPU:0, one launch (start us, length us, event | category | flops | bytes accessed | tf_op | source)
XLA Modules:
  0.0 371.3 jit_solution(6052622128554783701)
XLA Ops:
  10.3 5.1 %collective-permute-start.1 = (bf16[32,3712]{1,0:T(8,128)(2,1)S(1)}, bf16[32,3712]{1,0:T(8,128)(2,1)S(1)}, u32[]{:S(2)}, u32[]{:S(2)}) collective-permute-start(bf16[32,3712]{1,0:T(8,128)(2,1)S(1)} %copy.58), channel_id=1, source_target_pairs={{0,30},{2,0},{4,2},{6,4},{8,6},{10,8},{12,10},{14,12},{16,14},{18,... | collective-permute-start | bytes 712712 | tf_op jit(solution)/shard_map/ppermute | solution.py:51
  19.2 4.4 %collective-permute-start.3 = (bf16[32,3712]{1,0:T(8,128)(2,1)S(1)}, bf16[32,3712]{1,0:T(8,128)(2,1)S(1)}, u32[]{:S(2)}, u32[]{:S(2)}) collective-permute-start(bf16[32,3712]{1,0:T(8,128)(2,1)S(1)} %collective-permute-done.1), channel_id=1, source_target_pairs={{0,30},{2,0},{4,2},{6,4},{8,6},{10,8},{12,10},{14,12},{16,14},{18,... | collective-permute-start | bytes 712712 | tf_op jit(solution)/shard_map/ppermute | solution.py:51
  23.6 3.9 %collective-permute-done.2 = bf16[32,3712]{1,0:T(8,128)(2,1)S(1)} collective-permute-done((bf16[32,3712]{1,0:T(8,128)(2,1)S(1)}, bf16[32,3712]{1,0:T(8,128)(2,1)S(1)}, u32[]{:S(2)}, u32[]{:S(2)}) %collective-permute-start.2) | collective-permute-done | bytes 237600 | tf_op jit(solution)/shard_map/ppermute | solution.py:48
  27.5 4.4 %collective-permute-start.5 = (bf16[32,3712]{1,0:T(8,128)(2,1)S(1)}, bf16[32,3712]{1,0:T(8,128)(2,1)S(1)}, u32[]{:S(2)}, u32[]{:S(2)}) collective-permute-start(bf16[32,3712]{1,0:T(8,128)(2,1)S(1)} %collective-permute-done.3), channel_id=1, source_target_pairs={{0,30},{2,0},{4,2},{6,4},{8,6},{10,8},{12,10},{14,12},{16,14},{18,... | collective-permute-start | bytes 712712 | tf_op jit(solution)/shard_map/ppermute | solution.py:51
  32.0 3.9 %collective-permute-done.4 = bf16[32,3712]{1,0:T(8,128)(2,1)S(1)} collective-permute-done((bf16[32,3712]{1,0:T(8,128)(2,1)S(1)}, bf16[32,3712]{1,0:T(8,128)(2,1)S(1)}, u32[]{:S(2)}, u32[]{:S(2)}) %collective-permute-start.4) | collective-permute-done | bytes 237600 | tf_op jit(solution)/shard_map/ppermute | solution.py:48
  35.9 4.4 %collective-permute-start.7 = (bf16[32,3712]{1,0:T(8,128)(2,1)S(1)}, bf16[32,3712]{1,0:T(8,128)(2,1)S(1)}, u32[]{:S(2)}, u32[]{:S(2)}) collective-permute-start(bf16[32,3712]{1,0:T(8,128)(2,1)S(1)} %collective-permute-done.5), channel_id=1, source_target_pairs={{0,30},{2,0},{4,2},{6,4},{8,6},{10,8},{12,10},{14,12},{16,14},{18,... | collective-permute-start | bytes 712712 | tf_op jit(solution)/shard_map/ppermute | solution.py:51
  40.3 3.9 %collective-permute-done.6 = bf16[32,3712]{1,0:T(8,128)(2,1)S(1)} collective-permute-done((bf16[32,3712]{1,0:T(8,128)(2,1)S(1)}, bf16[32,3712]{1,0:T(8,128)(2,1)S(1)}, u32[]{:S(2)}, u32[]{:S(2)}) %collective-permute-start.6) | collective-permute-done | bytes 237600 | tf_op jit(solution)/shard_map/ppermute | solution.py:48
  44.2 4.4 %collective-permute-start.9 = (bf16[32,3712]{1,0:T(8,128)(2,1)S(1)}, bf16[32,3712]{1,0:T(8,128)(2,1)S(1)}, u32[]{:S(2)}, u32[]{:S(2)}) collective-permute-start(bf16[32,3712]{1,0:T(8,128)(2,1)S(1)} %collective-permute-done.7), channel_id=1, source_target_pairs={{0,30},{2,0},{4,2},{6,4},{8,6},{10,8},{12,10},{14,12},{16,14},{18,... | collective-permute-start | bytes 712712 | tf_op jit(solution)/shard_map/ppermute | solution.py:51
  48.7 3.9 %collective-permute-done.8 = bf16[32,3712]{1,0:T(8,128)(2,1)S(1)} collective-permute-done((bf16[32,3712]{1,0:T(8,128)(2,1)S(1)}, bf16[32,3712]{1,0:T(8,128)(2,1)S(1)}, u32[]{:S(2)}, u32[]{:S(2)}) %collective-permute-start.8) | collective-permute-done | bytes 237600 | tf_op jit(solution)/shard_map/ppermute | solution.py:48
  52.6 4.5 %collective-permute-start.11 = (bf16[32,3712]{1,0:T(8,128)(2,1)S(1)}, bf16[32,3712]{1,0:T(8,128)(2,1)S(1)}, u32[]{:S(2)}, u32[]{:S(2)}) collective-permute-start(bf16[32,3712]{1,0:T(8,128)(2,1)S(1)} %collective-permute-done.9), channel_id=1, source_target_pairs={{0,30},{2,0},{4,2},{6,4},{8,6},{10,8},{12,10},{14,12},{16,14},{18,... | collective-permute-start | bytes 712712 | tf_op jit(solution)/shard_map/ppermute | solution.py:51
  57.1 3.8 %collective-permute-done.10 = bf16[32,3712]{1,0:T(8,128)(2,1)S(1)} collective-permute-done((bf16[32,3712]{1,0:T(8,128)(2,1)S(1)}, bf16[32,3712]{1,0:T(8,128)(2,1)S(1)}, u32[]{:S(2)}, u32[]{:S(2)}) %collective-permute-start.10) | collective-permute-done | bytes 237600 | tf_op jit(solution)/shard_map/ppermute | solution.py:48
  60.9 4.5 %collective-permute-start.13 = (bf16[32,3712]{1,0:T(8,128)(2,1)S(1)}, bf16[32,3712]{1,0:T(8,128)(2,1)}, u32[]{:S(2)}, u32[]{:S(2)}) collective-permute-start(bf16[32,3712]{1,0:T(8,128)(2,1)S(1)} %collective-permute-done.11), channel_id=1, source_target_pairs={{0,30},{2,0},{4,2},{6,4},{8,6},{10,8},{12,10},{14,12},{16,14},{18,... | collective-permute-start | bytes 712712 | tf_op jit(solution)/shard_map/ppermute | solution.py:51
  65.4 3.8 %collective-permute-done.12 = bf16[32,3712]{1,0:T(8,128)(2,1)S(1)} collective-permute-done((bf16[32,3712]{1,0:T(8,128)(2,1)S(1)}, bf16[32,3712]{1,0:T(8,128)(2,1)S(1)}, u32[]{:S(2)}, u32[]{:S(2)}) %collective-permute-start.12) | collective-permute-done | bytes 237600 | tf_op jit(solution)/shard_map/ppermute | solution.py:48
  71.6 10.0 %dynamic_update_slice.48 = bf16[512,3712]{0,1:T(8,128)(2,1)} dynamic-update-slice(bf16[512,3712]{0,1:T(8,128)(2,1)} %broadcast_in_dim.57, bf16[32,3712]{0,1:T(8,128)(2,1)S(1)} %broadcast_dynamic-update-slice_fusion, s32[]{:T(128)S(6)} %select_n.131, s32[]{:T(128)} %constant.112.clone.1) | dynamic-update-slice | bytes 475140 | tf_op jit(solution)/shard_map/dynamic_update_slice | solution.py:43
  82.1 10.8 %dynamic_update_slice.49 = bf16[512,3712]{0,1:T(8,128)(2,1)} dynamic-update-slice(bf16[512,3712]{0,1:T(8,128)(2,1)} %dynamic_update_slice.48, bf16[32,3712]{0,1:T(8,128)(2,1)S(1)} %copy.59, s32[]{:T(128)S(6)} %select_n.133, s32[]{:T(128)} %constant.112.clone.1) | dynamic-update-slice | bytes 475140 | tf_op jit(solution)/shard_map/dynamic_update_slice | solution.py:49
  93.4 11.5 %dynamic_update_slice.50 = bf16[512,3712]{0,1:T(8,128)(2,1)} dynamic-update-slice(bf16[512,3712]{0,1:T(8,128)(2,1)} %dynamic_update_slice.49, bf16[32,3712]{0,1:T(8,128)(2,1)S(1)} %copy.61, s32[]{:T(128)S(6)} %select_n.135, s32[]{:T(128)} %constant.112.clone.1) | dynamic-update-slice | bytes 475140 | tf_op jit(solution)/shard_map/dynamic_update_slice | solution.py:52
  105.4 10.8 %dynamic_update_slice.51 = bf16[512,3712]{0,1:T(8,128)(2,1)} dynamic-update-slice(bf16[512,3712]{0,1:T(8,128)(2,1)} %dynamic_update_slice.50, bf16[32,3712]{0,1:T(8,128)(2,1)S(1)} %copy.62, s32[]{:T(128)S(6)} %select_n.137, s32[]{:T(128)} %constant.112.clone.1) | dynamic-update-slice | bytes 475140 | tf_op jit(solution)/shard_map/dynamic_update_slice | solution.py:49
  116.7 11.5 %dynamic_update_slice.52 = bf16[512,3712]{0,1:T(8,128)(2,1)} dynamic-update-slice(bf16[512,3712]{0,1:T(8,128)(2,1)} %dynamic_update_slice.51, bf16[32,3712]{0,1:T(8,128)(2,1)S(1)} %copy.63, s32[]{:T(128)S(6)} %select_n.139, s32[]{:T(128)} %constant.112.clone.1) | dynamic-update-slice | bytes 475140 | tf_op jit(solution)/shard_map/dynamic_update_slice | solution.py:52
  128.7 10.9 %dynamic_update_slice.53 = bf16[512,3712]{0,1:T(8,128)(2,1)} dynamic-update-slice(bf16[512,3712]{0,1:T(8,128)(2,1)} %dynamic_update_slice.52, bf16[32,3712]{0,1:T(8,128)(2,1)S(1)} %copy.64, s32[]{:T(128)S(6)} %select_n.141, s32[]{:T(128)} %constant.112.clone.1) | dynamic-update-slice | bytes 475140 | tf_op jit(solution)/shard_map/dynamic_update_slice | solution.py:49
  140.0 11.6 %dynamic_update_slice.54 = bf16[512,3712]{0,1:T(8,128)(2,1)} dynamic-update-slice(bf16[512,3712]{0,1:T(8,128)(2,1)} %dynamic_update_slice.53, bf16[32,3712]{0,1:T(8,128)(2,1)S(1)} %copy.65, s32[]{:T(128)S(6)} %select_n.143, s32[]{:T(128)} %constant.112.clone.1) | dynamic-update-slice | bytes 475140 | tf_op jit(solution)/shard_map/dynamic_update_slice | solution.py:52
  152.0 9.2 %dynamic_update_slice.55 = bf16[512,3712]{0,1:T(8,128)(2,1)} dynamic-update-slice(bf16[512,3712]{0,1:T(8,128)(2,1)} %dynamic_update_slice.54, bf16[32,3712]{0,1:T(8,128)(2,1)S(1)} %copy.66, s32[]{:T(128)S(6)} %select_n.145, s32[]{:T(128)} %constant.112.clone.1) | dynamic-update-slice | bytes 475140 | tf_op jit(solution)/shard_map/dynamic_update_slice | solution.py:49
  161.7 10.1 %dynamic_update_slice.56 = bf16[512,3712]{0,1:T(8,128)(2,1)} dynamic-update-slice(bf16[512,3712]{0,1:T(8,128)(2,1)} %dynamic_update_slice.55, bf16[32,3712]{0,1:T(8,128)(2,1)S(1)} %copy.67, s32[]{:T(128)S(6)} %select_n.147, s32[]{:T(128)} %constant.112.clone.1) | dynamic-update-slice | bytes 475140 | tf_op jit(solution)/shard_map/dynamic_update_slice | solution.py:52
  172.3 11.5 %dynamic_update_slice.57 = bf16[512,3712]{0,1:T(8,128)(2,1)} dynamic-update-slice(bf16[512,3712]{0,1:T(8,128)(2,1)} %dynamic_update_slice.56, bf16[32,3712]{0,1:T(8,128)(2,1)S(1)} %copy.68, s32[]{:T(128)S(6)} %select_n.149, s32[]{:T(128)} %constant.112.clone.1) | dynamic-update-slice | bytes 475140 | tf_op jit(solution)/shard_map/dynamic_update_slice | solution.py:49
  184.3 11.5 %dynamic_update_slice.58 = bf16[512,3712]{0,1:T(8,128)(2,1)} dynamic-update-slice(bf16[512,3712]{0,1:T(8,128)(2,1)} %dynamic_update_slice.57, bf16[32,3712]{0,1:T(8,128)(2,1)S(1)} %copy.69, s32[]{:T(128)S(6)} %select_n.151, s32[]{:T(128)} %constant.112.clone.1) | dynamic-update-slice | bytes 475140 | tf_op jit(solution)/shard_map/dynamic_update_slice | solution.py:52
  196.2 11.5 %dynamic_update_slice.59 = bf16[512,3712]{0,1:T(8,128)(2,1)} dynamic-update-slice(bf16[512,3712]{0,1:T(8,128)(2,1)} %dynamic_update_slice.58, bf16[32,3712]{0,1:T(8,128)(2,1)S(1)} %copy.70, s32[]{:T(128)S(6)} %select_n.153, s32[]{:T(128)} %constant.112.clone.1) | dynamic-update-slice | bytes 475140 | tf_op jit(solution)/shard_map/dynamic_update_slice | solution.py:49
  208.2 11.5 %dynamic_update_slice.60 = bf16[512,3712]{0,1:T(8,128)(2,1)} dynamic-update-slice(bf16[512,3712]{0,1:T(8,128)(2,1)} %dynamic_update_slice.59, bf16[32,3712]{0,1:T(8,128)(2,1)S(1)} %copy.71, s32[]{:T(128)S(6)} %select_n.155, s32[]{:T(128)} %constant.112.clone.1) | dynamic-update-slice | bytes 475140 | tf_op jit(solution)/shard_map/dynamic_update_slice | solution.py:52
  220.2 11.5 %dynamic_update_slice.61 = bf16[512,3712]{0,1:T(8,128)(2,1)} dynamic-update-slice(bf16[512,3712]{0,1:T(8,128)(2,1)} %dynamic_update_slice.60, bf16[32,3712]{0,1:T(8,128)(2,1)S(1)} %copy.72, s32[]{:T(128)S(6)} %select_n.157, s32[]{:T(128)} %constant.112.clone.1) | dynamic-update-slice | bytes 475140 | tf_op jit(solution)/shard_map/dynamic_update_slice | solution.py:49
  233.1 11.5 %dynamic_update_slice.62 = bf16[512,3712]{0,1:T(8,128)(2,1)} dynamic-update-slice(bf16[512,3712]{0,1:T(8,128)(2,1)} %dynamic_update_slice.61, bf16[32,3712]{0,1:T(8,128)(2,1)S(1)} %copy.73, s32[]{:T(128)S(6)} %select_n.159, s32[]{:T(128)} %constant.112.clone.1) | dynamic-update-slice | bytes 475140 | tf_op jit(solution)/shard_map/dynamic_update_slice | solution.py:52
  246.1 10.0 %dynamic_update_slice.63 = bf16[512,3712]{0,1:T(8,128)(2,1)} dynamic-update-slice(bf16[512,3712]{0,1:T(8,128)(2,1)} %dynamic_update_slice.62, bf16[32,3712]{0,1:T(8,128)(2,1)S(1)} %copy.74, s32[]{:T(128)S(6)} %select_n.161, s32[]{:T(128)} %constant.112.clone.1) | dynamic-update-slice | bytes 475140 | tf_op jit(solution)/shard_map/dynamic_update_slice | solution.py:49
  256.9 5.4 %fusion.2 = f32[512,512]{1,0:T(8,128)S(1)} fusion(bf16[1,3584,512]{2,1,0:T(8,128)(2,1)} %param.13, bf16[512,3712]{0,1:T(8,128)(2,1)} %dynamic_update_slice.63), kind=kOutput, calls=%fused_computation.3 | convolution fusion | flops 1879048192 | bytes 8388608 | tf_op jit(solution)/shard_map/dot_general | solution.py:62
  264.5 5.1 %convolution_multiply_fusion = f32[512,3584]{1,0:T(8,128)} fusion(bf16[1,512,3584]{2,1,0:T(8,128)(2,1)S(1)} %copy-done.12, f32[512]{0:T(512)S(1)} %fusion.19, f32[512,512]{1,0:T(8,128)S(1)} %fusion.2, f32[512,512]{1,0:T(8,128)S(1)} %fusion.4), kind=kOutput, calls=%fused_computation.1 | convolution fusion | flops 1882456064 | bytes 13109248 | tf_op jit(solution)/shard_map/dot_general | solution.py:64
  272.4 90.4 %reduce-scatter.2.cloned.1.call-done = f32[32,3584]{1,0:T(8,128)} async-done(((f32[512,3584]{1,0:T(8,128)}), f32[32,3584]{1,0:T(8,128)}) %reduce-scatter.2.cloned.1.call-update) | async-done | bytes 458768 | tf_op jit(solution)/shard_map/reduce_scatter | solution.py:66
  (80 shorter events, 25.2 us)
Async XLA Ops:
  7.2 263.1 %copy-start = (bf16[4,64,576]{2,1,0:T(8,128)(2,1)S(1)}, bf16[4,64,576]{2,1,0:T(8,128)(2,1)}, u32[]{:S(2)}) copy-start(bf16[4,64,576]{2,1,0:T(8,128)(2,1)} %param.15) | copy-start | bytes 884740
  7.2 355.6 %reduce-scatter.2.cloned.1.call-start = ((), (), s32[]{:S(2)}) async-start(), calls=%async_computation.1 | async-start | bytes 7798784 | tf_op jit(solution)/shard_map/reduce_scatter | solution.py:66
  9.8 9.4 %collective-permute-start = (bf16[32,3712]{1,0:T(8,128)(2,1)S(1)}, bf16[32,3712]{1,0:T(8,128)(2,1)S(1)}, u32[]{:S(2)}, u32[]{:S(2)}) collective-permute-start(bf16[32,3712]{1,0:T(8,128)(2,1)S(1)} %copy.58), channel_id=1, source_target_pairs={{0,2},{2,4},{4,6},{6,8},{8,10},{10,12},{12,14},{14,16},{16,18},{18... | collective-permute-start | bytes 712712 | tf_op jit(solution)/shard_map/ppermute | solution.py:48
  10.3 8.9 %collective-permute-start.1 = (bf16[32,3712]{1,0:T(8,128)(2,1)S(1)}, bf16[32,3712]{1,0:T(8,128)(2,1)S(1)}, u32[]{:S(2)}, u32[]{:S(2)}) collective-permute-start(bf16[32,3712]{1,0:T(8,128)(2,1)S(1)} %copy.58), channel_id=1, source_target_pairs={{0,30},{2,0},{4,2},{6,4},{8,6},{10,8},{12,10},{14,12},{16,14},{18,... | collective-permute-start | bytes 712712 | tf_op jit(solution)/shard_map/ppermute | solution.py:51
  19.2 8.3 %collective-permute-start.2 = (bf16[32,3712]{1,0:T(8,128)(2,1)S(1)}, bf16[32,3712]{1,0:T(8,128)(2,1)S(1)}, u32[]{:S(2)}, u32[]{:S(2)}) collective-permute-start(bf16[32,3712]{1,0:T(8,128)(2,1)S(1)} %collective-permute-done), channel_id=1, source_target_pairs={{0,2},{2,4},{4,6},{6,8},{8,10},{10,12},{12,14},{14,16},{16,18},{18... | collective-permute-start | bytes 712712 | tf_op jit(solution)/shard_map/ppermute | solution.py:48
  19.2 8.3 %collective-permute-start.3 = (bf16[32,3712]{1,0:T(8,128)(2,1)S(1)}, bf16[32,3712]{1,0:T(8,128)(2,1)S(1)}, u32[]{:S(2)}, u32[]{:S(2)}) collective-permute-start(bf16[32,3712]{1,0:T(8,128)(2,1)S(1)} %collective-permute-done.1), channel_id=1, source_target_pairs={{0,30},{2,0},{4,2},{6,4},{8,6},{10,8},{12,10},{14,12},{16,14},{18,... | collective-permute-start | bytes 712712 | tf_op jit(solution)/shard_map/ppermute | solution.py:51
  27.5 8.3 %collective-permute-start.4 = (bf16[32,3712]{1,0:T(8,128)(2,1)S(1)}, bf16[32,3712]{1,0:T(8,128)(2,1)S(1)}, u32[]{:S(2)}, u32[]{:S(2)}) collective-permute-start(bf16[32,3712]{1,0:T(8,128)(2,1)S(1)} %collective-permute-done.2), channel_id=1, source_target_pairs={{0,2},{2,4},{4,6},{6,8},{8,10},{10,12},{12,14},{14,16},{16,18},{18... | collective-permute-start | bytes 712712 | tf_op jit(solution)/shard_map/ppermute | solution.py:48
  27.5 8.3 %collective-permute-start.5 = (bf16[32,3712]{1,0:T(8,128)(2,1)S(1)}, bf16[32,3712]{1,0:T(8,128)(2,1)S(1)}, u32[]{:S(2)}, u32[]{:S(2)}) collective-permute-start(bf16[32,3712]{1,0:T(8,128)(2,1)S(1)} %collective-permute-done.3), channel_id=1, source_target_pairs={{0,30},{2,0},{4,2},{6,4},{8,6},{10,8},{12,10},{14,12},{16,14},{18,... | collective-permute-start | bytes 712712 | tf_op jit(solution)/shard_map/ppermute | solution.py:51
  35.9 8.3 %collective-permute-start.6 = (bf16[32,3712]{1,0:T(8,128)(2,1)S(1)}, bf16[32,3712]{1,0:T(8,128)(2,1)S(1)}, u32[]{:S(2)}, u32[]{:S(2)}) collective-permute-start(bf16[32,3712]{1,0:T(8,128)(2,1)S(1)} %collective-permute-done.4), channel_id=1, source_target_pairs={{0,2},{2,4},{4,6},{6,8},{8,10},{10,12},{12,14},{14,16},{16,18},{18... | collective-permute-start | bytes 712712 | tf_op jit(solution)/shard_map/ppermute | solution.py:48
  35.9 8.3 %collective-permute-start.7 = (bf16[32,3712]{1,0:T(8,128)(2,1)S(1)}, bf16[32,3712]{1,0:T(8,128)(2,1)S(1)}, u32[]{:S(2)}, u32[]{:S(2)}) collective-permute-start(bf16[32,3712]{1,0:T(8,128)(2,1)S(1)} %collective-permute-done.5), channel_id=1, source_target_pairs={{0,30},{2,0},{4,2},{6,4},{8,6},{10,8},{12,10},{14,12},{16,14},{18,... | collective-permute-start | bytes 712712 | tf_op jit(solution)/shard_map/ppermute | solution.py:51
  44.2 8.3 %collective-permute-start.8 = (bf16[32,3712]{1,0:T(8,128)(2,1)S(1)}, bf16[32,3712]{1,0:T(8,128)(2,1)S(1)}, u32[]{:S(2)}, u32[]{:S(2)}) collective-permute-start(bf16[32,3712]{1,0:T(8,128)(2,1)S(1)} %collective-permute-done.6), channel_id=1, source_target_pairs={{0,2},{2,4},{4,6},{6,8},{8,10},{10,12},{12,14},{14,16},{16,18},{18... | collective-permute-start | bytes 712712 | tf_op jit(solution)/shard_map/ppermute | solution.py:48
  44.2 8.3 %copy-start.3 = (bf16[32,3712]{1,0:T(8,128)(2,1)}, bf16[32,3712]{1,0:T(8,128)(2,1)S(1)}, u32[]{:S(2)}) copy-start(bf16[32,3712]{1,0:T(8,128)(2,1)S(1)} %collective-permute-done.7) | copy-start | bytes 712708
  44.2 8.3 %collective-permute-start.9 = (bf16[32,3712]{1,0:T(8,128)(2,1)S(1)}, bf16[32,3712]{1,0:T(8,128)(2,1)S(1)}, u32[]{:S(2)}, u32[]{:S(2)}) collective-permute-start(bf16[32,3712]{1,0:T(8,128)(2,1)S(1)} %collective-permute-done.7), channel_id=1, source_target_pairs={{0,30},{2,0},{4,2},{6,4},{8,6},{10,8},{12,10},{14,12},{16,14},{18,... | collective-permute-start | bytes 712712 | tf_op jit(solution)/shard_map/ppermute | solution.py:51
  52.6 16.7 %copy-start.5 = (bf16[32,3712]{1,0:T(8,128)(2,1)}, bf16[32,3712]{1,0:T(8,128)(2,1)S(1)}, u32[]{:S(2)}) copy-start(bf16[32,3712]{1,0:T(8,128)(2,1)S(1)} %collective-permute-done.8) | copy-start | bytes 712708
  52.6 8.3 %collective-permute-start.10 = (bf16[32,3712]{1,0:T(8,128)(2,1)S(1)}, bf16[32,3712]{1,0:T(8,128)(2,1)S(1)}, u32[]{:S(2)}, u32[]{:S(2)}) collective-permute-start(bf16[32,3712]{1,0:T(8,128)(2,1)S(1)} %collective-permute-done.8), channel_id=1, source_target_pairs={{0,2},{2,4},{4,6},{6,8},{8,10},{10,12},{12,14},{14,16},{16,18},{18... | collective-permute-start | bytes 712712 | tf_op jit(solution)/shard_map/ppermute | solution.py:48
  52.6 16.7 %copy-start.7 = (bf16[32,3712]{1,0:T(8,128)(2,1)}, bf16[32,3712]{1,0:T(8,128)(2,1)S(1)}, u32[]{:S(2)}) copy-start(bf16[32,3712]{1,0:T(8,128)(2,1)S(1)} %collective-permute-done.9) | copy-start | bytes 712708
  52.6 8.3 %collective-permute-start.11 = (bf16[32,3712]{1,0:T(8,128)(2,1)S(1)}, bf16[32,3712]{1,0:T(8,128)(2,1)S(1)}, u32[]{:S(2)}, u32[]{:S(2)}) collective-permute-start(bf16[32,3712]{1,0:T(8,128)(2,1)S(1)} %collective-permute-done.9), channel_id=1, source_target_pairs={{0,30},{2,0},{4,2},{6,4},{8,6},{10,8},{12,10},{14,12},{16,14},{18,... | collective-permute-start | bytes 712712 | tf_op jit(solution)/shard_map/ppermute | solution.py:51
  60.9 8.4 %copy-start.9 = (bf16[32,3712]{1,0:T(8,128)(2,1)}, bf16[32,3712]{1,0:T(8,128)(2,1)S(1)}, u32[]{:S(2)}) copy-start(bf16[32,3712]{1,0:T(8,128)(2,1)S(1)} %collective-permute-done.10) | copy-start | bytes 712708
  60.9 8.3 %collective-permute-start.12 = (bf16[32,3712]{1,0:T(8,128)(2,1)S(1)}, bf16[32,3712]{1,0:T(8,128)(2,1)S(1)}, u32[]{:S(2)}, u32[]{:S(2)}) collective-permute-start(bf16[32,3712]{1,0:T(8,128)(2,1)S(1)} %collective-permute-done.10), channel_id=1, source_target_pairs={{0,2},{2,4},{4,6},{6,8},{8,10},{10,12},{12,14},{14,16},{16,18},{18... | collective-permute-start | bytes 712712 | tf_op jit(solution)/shard_map/ppermute | solution.py:48
  60.9 170.8 %collective-permute-start.13 = (bf16[32,3712]{1,0:T(8,128)(2,1)S(1)}, bf16[32,3712]{1,0:T(8,128)(2,1)}, u32[]{:S(2)}, u32[]{:S(2)}) collective-permute-start(bf16[32,3712]{1,0:T(8,128)(2,1)S(1)} %collective-permute-done.11), channel_id=1, source_target_pairs={{0,30},{2,0},{4,2},{6,4},{8,6},{10,8},{12,10},{14,12},{16,14},{18,... | collective-permute-start | bytes 712712 | tf_op jit(solution)/shard_map/ppermute | solution.py:51
  69.2 175.4 %collective-permute-start.14 = (bf16[32,3712]{1,0:T(8,128)(2,1)S(1)}, bf16[32,3712]{1,0:T(8,128)(2,1)}, u32[]{:S(2)}, u32[]{:S(2)}) collective-permute-start(bf16[32,3712]{1,0:T(8,128)(2,1)S(1)} %collective-permute-done.12), channel_id=1, source_target_pairs={{0,2},{2,4},{4,6},{6,8},{8,10},{10,12},{12,14},{14,16},{16,18},{18... | collective-permute-start | bytes 712712 | tf_op jit(solution)/shard_map/ppermute | solution.py:48
  128.7 32.6 %copy-start.4 = (bf16[32,3712]{1,0:T(8,128)(2,1)S(1)}, bf16[32,3712]{1,0:T(8,128)(2,1)}, u32[]{:S(2)}) copy-start(bf16[32,3712]{1,0:T(8,128)(2,1)} %copy-done.3) | copy-start | bytes 712708
  140.0 31.8 %copy-start.6 = (bf16[32,3712]{1,0:T(8,128)(2,1)S(1)}, bf16[32,3712]{1,0:T(8,128)(2,1)}, u32[]{:S(2)}) copy-start(bf16[32,3712]{1,0:T(8,128)(2,1)} %copy-done.5) | copy-start | bytes 712708
  152.0 31.8 %copy-start.8 = (bf16[32,3712]{1,0:T(8,128)(2,1)S(1)}, bf16[32,3712]{1,0:T(8,128)(2,1)}, u32[]{:S(2)}) copy-start(bf16[32,3712]{1,0:T(8,128)(2,1)} %copy-done.7) | copy-start | bytes 712708
  161.7 34.1 %copy-start.10 = (bf16[32,3712]{1,0:T(8,128)(2,1)S(1)}, bf16[32,3712]{1,0:T(8,128)(2,1)}, u32[]{:S(2)}) copy-start(bf16[32,3712]{1,0:T(8,128)(2,1)} %copy-done.9) | copy-start | bytes 712708
  256.9 5.4 %copy-start.1 = (bf16[512,3712]{0,1:T(8,128)(2,1)S(1)}, bf16[512,3712]{0,1:T(8,128)(2,1)}, u32[]{:S(2)}) copy-start(bf16[512,3712]{0,1:T(8,128)(2,1)} %dynamic_update_slice.63) | copy-start | bytes 11403268
  256.9 5.4 %copy-start.11 = (bf16[1,3584,512]{2,1,0:T(8,128)(2,1)S(1)}, bf16[1,3584,512]{2,1,0:T(8,128)(2,1)}, u32[]{:S(2)}) copy-start(bf16[1,3584,512]{2,1,0:T(8,128)(2,1)} %param.12) | copy-start | bytes 11010052
  262.3 2.2 copy-start.12
  269.6 0.7 copy-start.13
  269.6 1.1 copy-start.2
Sparse Core Ops, SparseCore 0:
  269.7 93.0 reduce-scatter.1
